TPU v7x, 256 devices: a whole 4x4x8 slice. The times are simulated.
256 devices in a mesh: section: 4 (over z_hi, core), ep: 64 (over y, x, z_lo).
Axes of the slice: x: 4, y: 4, z: 8 (z_hi: 2, z_lo: 4; z = z_hi * 4 + z_lo), core: 2. Of those that a mesh axis runs over, the one named last changes fastest.
Arguments:
- tokens: bfloat16 [4, 8192, 4096], P('section', 'ep'), may hold values from -6 to 6
- routes: int32 [4, 8192, 8], P('section', 'ep'), may hold values from 0 to 127, as said below
- router_weights: float32 [4, 8192, 8], P('section', 'ep'), may hold values from 0.25 to 1
- w_gate: bfloat16 [4, 64, 4096, 384], P('section', 'ep'), may hold values from -0.09375 to 0.09375
- w_up: bfloat16 [4, 64, 4096, 384], P('section', 'ep'), may hold values from -0.09375 to 0.09375
- w_down: bfloat16 [4, 64, 384, 4096], P('section', 'ep'), may hold values from -0.15625 to 0.15625
- w_query: bfloat16 [4, 4096, 1024], P('section', 'ep'), may hold values from -0.09375 to 0.09375
- w_keyval: bfloat16 [4, 4096, 256], P('section', 'ep'), may hold values from -0.09375 to 0.09375
- gain_query: float32 [4, 128], P('section'), may hold values from 0.8 to 2
- gain_key: float32 [4, 128], P('section'), may hold values from 0.8 to 2
- segment_ids: int32 [4, 8192], P('section', 'ep'), may hold values from 0 to 31, never falling along the last dimension, each value on 1 to 512 neighbouring positions
Outputs:
- layer_out: bfloat16 [4, 8192, 4096], P('section', 'ep')
- attended: bfloat16 [4, 8192, 1024], P('section', 'ep')
Inputs may be any that keep to these rules, and one draw needn't show every extreme that they name: `routes`: each token names 8 different experts, at most one of them below 16. Among the tokens of one device (aligned blocks of 128 rows in each section) no expert below 16 is named by more than 8 of them, and in each section one expert below 16 is named by exactly 8 tokens of every block. `segment_ids`: along each section's tokens the reaction numbers never fall; each reaction spans 1 to 512 tokens and one spans exactly 512.
All inputs are finite; a program needn't handle non-finite values.
Results may differ from a plain program's by a relative error of at most 0.018.
Values may be sent and summed in bfloat16 or wider, within the bound.
No kernel may reach another device: no remote copies, remote signals or barrier semaphores. Data moves between devices by JAX's collectives and lax.ppermute only.
A program may use at most 128 MiB of HBM per device.

v0:
```python
import math
import jax
import jax.numpy as jnp
from jax import lax
from jax.sharding import PartitionSpec as P

OWNERS = 4
SEG_MOST = 512
EPSILON = 1e-06
ROPE_BASE = 1000000.0
FAR_INDEX = 1073741824


def passed_along(block, axis, distance):
    devices = range(lax.axis_size(axis))
    route = [((i - distance) % len(devices), i) for i in devices]
    return lax.ppermute(block, axis, route)


def prefix(shard, axis, combine, identity):
    length, mine = (lax.axis_size(axis), lax.axis_index(axis))
    everything = jax.tree.map(lambda part: lax.all_gather(part, axis), shard)
    start = jax.tree.map(
        lambda part, zero: jnp.broadcast_to(jnp.asarray(zero, part.dtype), part.shape),
        shard,
        identity,
    )

    def step(k, before):
        reached = k < mine
        new = combine(before, jax.tree.map(lambda part: part[k], everything))
        return jax.tree.map(lambda a, b: jnp.where(reached, a, b), new, before)

    return lax.fori_loop(0, length, step, start)


def passed_along_2(value, axis, steps):
    count = lax.axis_size(axis)
    leading, last = (max(0, -steps), min(count, count - steps))
    return lax.ppermute(value, axis, [(source, source + steps) for source in range(leading, last)])


def rms_rows(values):
    return values * lax.rsqrt(jnp.mean(values * values, axis=-1, keepdims=True) + EPSILON)


def rotary(values, position):
    half_count = values.shape[-1] // 2
    frequency = ROPE_BASE ** (-(jnp.arange(half_count, dtype=jnp.float32) * 2.0) / values.shape[-1])
    angles = position.astype(jnp.float32)[:, None] * frequency[None, :]
    cosine = jnp.concatenate([jnp.cos(angles), jnp.cos(angles)], axis=-1)[:, None, :]
    sine = jnp.concatenate([jnp.sin(angles), jnp.sin(angles)], axis=-1)[:, None, :]
    turned = jnp.concatenate([-values[..., half_count:], values[..., :half_count]], axis=-1)
    return values * cosine + turned * sine


def feed_forward(row_block, gate_part, up_part, down_part):
    gate_proj = jnp.dot(row_block, gate_part, preferred_element_type=jnp.float32)
    up_proj = jnp.dot(row_block, up_part, preferred_element_type=jnp.float32)
    activated = (jax.nn.silu(gate_proj) * up_proj).astype(jnp.bfloat16)
    return jnp.dot(activated, down_part, preferred_element_type=jnp.float32)


def keep_later(earlier, later):
    same_id = earlier[0] == later[0]
    newer_id = later[0] > earlier[0]
    start_at = jnp.where(
        same_id, jnp.minimum(earlier[1], later[1]), jnp.where(newer_id, later[1], earlier[1])
    )
    return (jnp.maximum(earlier[0], later[0]), start_at)


def on_device(
    tokens,
    routes,
    router_weights,
    w_gate,
    w_up,
    w_down,
    w_query,
    w_keyval,
    gain_query,
    gain_key,
    segment_ids,
):
    device_count = lax.axis_size("ep")
    expert_count = device_count // OWNERS
    token_count = tokens.shape[1]
    model_width = tokens.shape[2]
    capacity = OWNERS * max(1, token_count // device_count)
    wide_tokens = tokens[0].astype(jnp.float32)
    normed = rms_rows(wide_tokens).astype(jnp.bfloat16)
    inside = routes[0] < expert_count
    has_route = jnp.any(inside, axis=-1)
    chosen = jnp.sum(jnp.where(inside, routes[0], 0), axis=-1)
    weight_kept = jnp.sum(jnp.where(inside, router_weights[0], 0.0), axis=-1)
    expert_ids = jnp.arange(expert_count, dtype=jnp.int32)
    member = ((chosen[:, None] == expert_ids[None, :]) & has_route[:, None]).astype(jnp.int32)
    rank_within = jnp.sum((jnp.cumsum(member, axis=0) - member) * member, axis=-1)
    slot_index = jnp.where(has_route, chosen * capacity + rank_within, -1)
    slot_ids = jnp.arange(expert_count * capacity, dtype=jnp.int32)
    placing = (slot_ids[:, None] == slot_index[None, :]).astype(jnp.bfloat16)
    packed = jnp.dot(placing, normed, preferred_element_type=jnp.float32).astype(jnp.bfloat16)
    gate_part = w_gate[0, 0]
    up_part = w_up[0, 0]
    down_part = w_down[0, 0]
    spread = jnp.broadcast_to(
        packed.reshape(expert_count, 1, capacity, model_width),
        (expert_count, OWNERS, capacity, model_width),
    ).reshape(device_count, capacity, model_width)
    received = lax.all_to_all(spread, "ep", split_axis=0, concat_axis=0, tiled=True)
    partial_out = feed_forward(
        received.reshape(-1, model_width), gate_part, up_part, down_part
    ).reshape(received.shape)
    returned_rows = lax.all_to_all(
        partial_out.astype(jnp.bfloat16), "ep", split_axis=0, concat_axis=0, tiled=True
    ).astype(partial_out.dtype)
    merged = jnp.sum(
        returned_rows.reshape(expert_count, OWNERS, capacity, model_width), axis=1
    ).reshape(expert_count * capacity, model_width)
    fetched_rows = jnp.take(merged, jnp.maximum(slot_index, 0), axis=0)
    expert_out = jnp.where(has_route[:, None], fetched_rows, 0.0)
    layer_out = (wide_tokens + weight_kept[:, None] * expert_out).astype(jnp.bfloat16)
    arrived = passed_along(layer_out, "section", 1)
    lifted = rms_rows(arrived.astype(jnp.float32)).astype(jnp.bfloat16)
    head_dim = gain_query.shape[-1]
    query_width = w_query.shape[-1]
    head_count = query_width // head_dim
    query_raw = jnp.dot(
        lifted,
        lax.all_gather(w_query[0], "ep", axis=0, tiled=True),
        preferred_element_type=jnp.float32,
    )
    keyval_raw = jnp.dot(
        lifted,
        lax.all_gather(w_keyval[0], "ep", axis=0, tiled=True),
        preferred_element_type=jnp.float32,
    )
    segment_row = segment_ids[0]
    first_index = lax.axis_index("ep") * token_count
    global_index = first_index + jnp.arange(token_count, dtype=jnp.int32)
    reach = (SEG_MOST - 1) // token_count + 1
    key_index = (
        first_index - reach * token_count + jnp.arange((reach + 1) * token_count, dtype=jnp.int32)
    )
    segment_pieces = []
    for distance in range(1, reach + 1):
        segment_pieces.append(passed_along_2(segment_row, "ep", distance))
    window_segment = jnp.concatenate(segment_pieces[::-1] + [segment_row], axis=0)
    window_segment = jnp.where(key_index >= 0, window_segment, -1)
    same_segment = window_segment[None, :] == segment_row[:, None]
    start_index = jnp.min(jnp.where(same_segment, key_index[None, :], FAR_INDEX), axis=1)
    position = global_index - start_index
    query = rotary(
        rms_rows(query_raw.reshape(token_count, head_count, head_dim)) * gain_query[0], position
    ).astype(jnp.bfloat16)
    key_part = rotary(rms_rows(keyval_raw[:, None, :head_dim]) * gain_key[0], position)[
        :, 0
    ].astype(jnp.bfloat16)
    value_part = keyval_raw[:, head_dim:].astype(jnp.bfloat16)
    key_value = jnp.concatenate([key_part, value_part], axis=-1)
    earlier_pieces = []
    for distance in range(1, reach + 1):
        earlier_pieces.append(passed_along_2(key_value, "ep", distance))
    window = jnp.concatenate(earlier_pieces[::-1] + [key_value], axis=0)
    score_scale = 1.0 / math.sqrt(head_dim)
    scores = (
        jnp.einsum("thd,kd->thk", query, window[:, :head_dim], preferred_element_type=jnp.float32)
        * score_scale
    )
    allowed = (same_segment & (key_index[None, :] <= global_index[:, None]))[:, None, :]
    probabilities = jnp.where(allowed, jnp.exp(scores), 0.0)
    total_mass = jnp.sum(probabilities, axis=-1)
    mixed = jnp.einsum(
        "thk,kd->thd",
        probabilities.astype(jnp.bfloat16),
        window[:, head_dim:],
        preferred_element_type=jnp.float32,
    )
    attended = (
        (mixed / total_mass[..., None]).astype(jnp.bfloat16).reshape(token_count, query_width)
    )
    return (layer_out[None], attended[None])


def solution(mesh):
    in_specs = (
        P("section", "ep", None),
        P("section", "ep", None),
        P("section", "ep", None),
        P("section", "ep", None, None),
        P("section", "ep", None, None),
        P("section", "ep", None, None),
        P("section", "ep", None),
        P("section", "ep", None),
        P("section", None),
        P("section", None),
        P("section", "ep"),
    )
    out_specs = (P("section", "ep", None), P("section", "ep", None))
    return jax.shard_map(
        on_device, mesh=mesh, in_specs=in_specs, out_specs=out_specs, check_vma=False
    )
```

profile of v0, /device:TPU:32, one launch (start us, length us, event | category | flops | bytes accessed | tf_op | source)
XLA Modules:
  0.0 803.5 jit_solution(15481423913225358977)
XLA Ops:
  7.2 0.9 fusion.83
  8.0 0.8 fusion.79
  8.8 1.5 fusion.15
  10.8 1.7 fusion.2
  12.6 2.5 broadcast_in_dim.108
  15.0 11.8 %all-to-all-start = ((bf16[64,8,4096]{2,1,0:T(8,128)(2,1)}), bf16[64,8,4096]{2,1,0:T(8,128)(2,1)}, u32[]{:S(2)}, u32[]{:S(2)}) async-start(bf16[64,8,4096]{2,1,0:T(8,128)(2,1)} %bitcast.115), calls=%async_computation | async-start | bytes 8388608 | tf_op jit(solution)/shard_map/all_to_all | solution.py:111
  26.9 0.7 all-gather.7.cloned.1.call-update
  27.7 0.7 all-gather.5.cloned.1.call-update
  28.4 108.3 %all-to-all-done = bf16[64,8,4096]{2,1,0:T(8,128)(2,1)} async-done(((bf16[64,8,4096]{2,1,0:T(8,128)(2,1)}), bf16[64,8,4096]{2,1,0:T(8,128)(2,1)}, u32[]{:S(2)}, u32[]{:S(2)}) %all-to-all-start) | async-done | bytes 4194336 | tf_op jit(solution)/shard_map/all_to_all | solution.py:111
  136.7 6.4 fusion.5
  143.0 9.7 %convolution_convert_fusion = bf16[64,8,4096]{2,1,0:T(8,128)(2,1)} fusion(bf16[1,1,384,4096]{3,2,1,0:T(8,128)(2,1)S(1)} %copy-done, bf16[1,1,4096,384]{3,2,1,0:T(8,128)(2,1)} %param.15, bf16[64,8,4096]{2,1,0:T(8,128)(2,1)} %all-to-all-done, f32[512,384]{1,0:T(8,128)} %fusion.5), kind=kOutput, calls=%fused_computation.4 | convolution fusion | flops 3224502272 | bytes 15466496 | tf_op jit(solution)/shard_map/dot_general | solution.py:61
  152.8 6.9 all-to-all-start.1
  159.7 3.4 collective-permute-start
  163.0 3.4 collective-permute-start.1
  166.4 4.3 collective-permute-start.2
  170.7 4.3 collective-permute-start.3
  175.1 1.2 collective-permute-done
  176.3 32.1 %collective-permute-done.1 = s32[128]{0:T(128)S(1)} collective-permute-done((s32[128]{0:T(128)S(1)}, s32[128]{0:T(128)S(1)}, u32[]{:S(2)}, u32[]{:S(2)}) %collective-permute-start.1) | collective-permute-done | bytes 544 | tf_op jit(solution)/shard_map/ppermute | solution.py:40
  208.4 53.8 %collective-permute-done.2 = s32[128]{0:T(128)S(1)} collective-permute-done((s32[128]{0:T(128)S(1)}, s32[128]{0:T(128)S(1)}, u32[]{:S(2)}, u32[]{:S(2)}) %collective-permute-start.2) | collective-permute-done | bytes 544 | tf_op jit(solution)/shard_map/ppermute | solution.py:40
  262.8 7.9 all-to-all-done.1
  270.7 4.5 convert_reduce_fusion
  275.1 5.0 gather_fusion
  280.2 2.6 fusion.17
  283.2 1.6 fusion.18
  284.8 27.8 %collective-permute-done.4 = bf16[128,4096]{1,0:T(8,128)(2,1)S(1)} collective-permute-done((bf16[128,4096]{1,0:T(8,128)(2,1)S(1)}, bf16[128,4096]{1,0:T(8,128)(2,1)S(1)}, u32[]{:S(2)}, u32[]{:S(2)}) %collective-permute-start.4) | collective-permute-done | bytes 1048608 | tf_op jit(solution)/shard_map/ppermute | solution.py:17
  312.5 1.1 copy-done.3
  313.9 78.5 %all-gather.7.cloned.1.call-done = bf16[1,4096,256]{2,1,0:T(8,128)(2,1)} async-done(((bf16[1,64,256]{2,1,0:T(8,128)(2,1)}), bf16[1,4096,256]{2,1,0:T(8,128)(2,1)}) %all-gather.7.cloned.1.call-update) | async-done | bytes 2097168 | tf_op jit(solution)/shard_map/all_gather | solution.py:136
  392.4 2.4 fusion.21
  395.2 0.8 fusion.73
  396.0 1.9 collective-permute-start.5
  397.9 1.9 collective-permute-start.6
  399.8 1.9 collective-permute-start.7
  401.7 5.2 collective-permute-start.8
  406.9 373.2 %all-gather.5.cloned.1.call-done = bf16[1,4096,1024]{2,1,0:T(8,128)(2,1)} async-done(((bf16[1,64,1024]{2,1,0:T(8,128)(2,1)}), bf16[1,4096,1024]{2,1,0:T(8,128)(2,1)}) %all-gather.5.cloned.1.call-update) | async-done | bytes 8388624 | tf_op jit(solution)/shard_map/all_gather | solution.py:131
  780.1 5.0 fusion.43
  785.3 0.8 copy-done.4
  786.3 0.7 copy.19
  786.9 1.3 add_rsqrt_fusion
  788.2 0.8 copy.20
  789.0 1.3 multiply_multiply_fusion
  790.6 0.3 fusion.64
  790.9 0.8 constant_dynamic-update-slice_fusion.5
  791.8 0.8 constant_dynamic-update-slice_fusion.4
  792.6 0.8 constant_dynamic-update-slice_fusion.3
  793.5 0.8 constant_dynamic-update-slice_fusion.2
  794.3 0.8 fusion.13
  795.2 0.6 fusion.46
  795.8 0.9 copy.23
  (63 shorter events, 2.7 us)
Async XLA Ops:
  7.2 135.9 %copy-start = (bf16[1,1,384,4096]{3,2,1,0:T(8,128)(2,1)S(1)}, bf16[1,1,384,4096]{3,2,1,0:T(8,128)(2,1)}, u32[]{:S(2)}) copy-start(bf16[1,1,384,4096]{3,2,1,0:T(8,128)(2,1)} %param.16) | copy-start | bytes 9437188
  15.0 121.6 %all-to-all-start = ((bf16[64,8,4096]{2,1,0:T(8,128)(2,1)}), bf16[64,8,4096]{2,1,0:T(8,128)(2,1)}, u32[]{:S(2)}, u32[]{:S(2)}) async-start(bf16[64,8,4096]{2,1,0:T(8,128)(2,1)} %bitcast.115), calls=%async_computation | async-start | bytes 8388608 | tf_op jit(solution)/shard_map/all_to_all | solution.py:111
  26.9 365.5 %all-gather.7.cloned.1.call-start = ((), (), s32[]{:S(2)}) async-start(), calls=%async_computation.3 | async-start | bytes 2129920 | tf_op jit(solution)/shard_map/all_gather | solution.py:136
  27.6 752.5 %all-gather.5.cloned.1.call-start = ((), (), s32[]{:S(2)}) async-start(), calls=%async_computation.2 | async-start | bytes 8519680 | tf_op jit(solution)/shard_map/all_gather | solution.py:131
  152.8 6.9 copy-start.10
  152.8 22.3 %copy-start.6 = (s32[1,128,8]{1,2,0:T(8,128)S(1)}, s32[1,128,8]{1,2,0:T(8,128)}, u32[]{:S(2)}) copy-start(s32[1,128,8]{1,2,0:T(8,128)} %param.12) | copy-start | bytes 12292
  152.8 22.3 %copy-start.8 = (f32[1,128,8]{1,2,0:T(8,128)S(1)}, f32[1,128,8]{1,2,0:T(8,128)}, u32[]{:S(2)}) copy-start(f32[1,128,8]{1,2,0:T(8,128)} %param.13) | copy-start | bytes 12292
  152.8 117.9 %all-to-all-start.1 = ((bf16[64,8,4096]{2,1,0:T(8,128)(2,1)}), bf16[64,8,4096]{2,1,0:T(8,128)(2,1)}, u32[]{:S(2)}, u32[]{:S(2)}) async-start(bf16[64,8,4096]{2,1,0:T(8,128)(2,1)} %convolution_convert_fusion), calls=%async_computation.1 | async-start | bytes 8388608 | tf_op jit(solution)/shard_map/all_to_all | solution.py:115
  159.7 16.6 %collective-permute-start = (s32[128]{0:T(128)S(1)}, s32[128]{0:T(128)S(1)}, u32[]{:S(2)}, u32[]{:S(2)}) collective-permute-start(s32[128]{0:T(128)S(1)} %bitcast.120), channel_id=1, source_target_pairs={{0,4},{1,5},{2,6},{3,7},{4,8},{5,9},{6,10},{7,11},{8,12},{9,13},{1... | collective-permute-start | bytes 1544 | tf_op jit(solution)/shard_map/ppermute | solution.py:40
  163.0 45.4 %collective-permute-start.1 = (s32[128]{0:T(128)S(1)}, s32[128]{0:T(128)S(1)}, u32[]{:S(2)}, u32[]{:S(2)}) collective-permute-start(s32[128]{0:T(128)S(1)} %bitcast.121), channel_id=1, source_target_pairs={{0,3},{1,4},{2,5},{3,6},{4,7},{5,8},{6,9},{7,10},{8,11},{9,12},{10... | collective-permute-start | bytes 1544 | tf_op jit(solution)/shard_map/ppermute | solution.py:40
  166.4 95.8 %collective-permute-start.2 = (s32[128]{0:T(128)S(1)}, s32[128]{0:T(128)S(1)}, u32[]{:S(2)}, u32[]{:S(2)}) collective-permute-start(s32[128]{0:T(128)S(1)} %bitcast.122), channel_id=1, source_target_pairs={{0,2},{1,3},{2,4},{3,5},{4,6},{5,7},{6,8},{7,9},{8,10},{9,11},{10,... | collective-permute-start | bytes 1544 | tf_op jit(solution)/shard_map/ppermute | solution.py:40
  170.7 91.6 %collective-permute-start.3 = (s32[128]{0:T(128)S(1)}, s32[128]{0:T(128)S(1)}, u32[]{:S(2)}, u32[]{:S(2)}) collective-permute-start(s32[128]{0:T(128)S(1)} %bitcast.123), channel_id=1, source_target_pairs={{0,1},{1,2},{2,3},{3,4},{4,5},{5,6},{6,7},{7,8},{8,9},{9,10},{10,1... | collective-permute-start | bytes 1544 | tf_op jit(solution)/shard_map/ppermute | solution.py:40
  280.2 3.0 copy-start.1
  280.2 3.0 copy-start.2
  282.8 29.8 %collective-permute-start.4 = (bf16[128,4096]{1,0:T(8,128)(2,1)S(1)}, bf16[128,4096]{1,0:T(8,128)(2,1)S(1)}, u32[]{:S(2)}, u32[]{:S(2)}) collective-permute-start(bf16[128,4096]{1,0:T(8,128)(2,1)S(1)} %fusion.17), channel_id=1, source_target_pairs={{192,0},{0,64},{64,128},{128,192},{193,1},{1,65},{65,129},{129,193... | collective-permute-start | bytes 3145736 | tf_op jit(solution)/shard_map/ppermute | solution.py:17
  284.8 110.2 %copy-start.11 = (f32[1,128]{1,0:T(1,128)S(1)}, f32[1,128]{1,0:T(1,128)}, u32[]{:S(2)}) copy-start(f32[1,128]{1,0:T(1,128)} %param.20) | copy-start | bytes 1540
  312.5 1.1 copy-start.3
  313.9 78.5 %copy-start.7 = (f32[128]{0:T(128)}, f32[128]{0:T(128)S(1)}, u32[]{:S(2)}) copy-start(f32[128]{0:T(128)S(1)} %add_rsqrt_fusion.2) | copy-start | bytes 1540
  396.0 394.9 %collective-permute-start.5 = (bf16[128,256]{1,0:T(8,128)(2,1)S(1)}, bf16[128,256]{1,0:T(8,128)(2,1)}, u32[]{:S(2)}, u32[]{:S(2)}) collective-permute-start(bf16[128,256]{1,0:T(8,128)(2,1)S(1)} %pad_maximum_fusion.2), channel_id=1, source_target_pairs={{0,4},{1,5},{2,6},{3,7},{4,8},{5,9},{6,10},{7,11},{8,12},{9,13},{1... | collective-permute-start | bytes 196616 | tf_op jit(solution)/shard_map/ppermute | solution.py:40
  397.9 393.9 %collective-permute-start.6 = (bf16[128,256]{1,0:T(8,128)(2,1)S(1)}, bf16[128,256]{1,0:T(8,128)(2,1)}, u32[]{:S(2)}, u32[]{:S(2)}) collective-permute-start(bf16[128,256]{1,0:T(8,128)(2,1)S(1)} %pad_maximum_fusion.2), channel_id=1, source_target_pairs={{0,3},{1,4},{2,5},{3,6},{4,7},{5,8},{6,9},{7,10},{8,11},{9,12},{10... | collective-permute-start | bytes 196616 | tf_op jit(solution)/shard_map/ppermute | solution.py:40
  399.8 392.8 %collective-permute-start.7 = (bf16[128,256]{1,0:T(8,128)(2,1)S(1)}, bf16[128,256]{1,0:T(8,128)(2,1)}, u32[]{:S(2)}, u32[]{:S(2)}) collective-permute-start(bf16[128,256]{1,0:T(8,128)(2,1)S(1)} %pad_maximum_fusion.2), channel_id=1, source_target_pairs={{0,2},{1,3},{2,4},{3,5},{4,6},{5,7},{6,8},{7,9},{8,10},{9,11},{10,... | collective-permute-start | bytes 196616 | tf_op jit(solution)/shard_map/ppermute | solution.py:40
  401.7 391.7 %collective-permute-start.8 = (bf16[128,256]{1,0:T(8,128)(2,1)S(1)}, bf16[128,256]{1,0:T(8,128)(2,1)}, u32[]{:S(2)}, u32[]{:S(2)}) collective-permute-start(bf16[128,256]{1,0:T(8,128)(2,1)S(1)} %pad_maximum_fusion.2), channel_id=1, source_target_pairs={{0,1},{1,2},{2,3},{3,4},{4,5},{5,6},{6,7},{7,8},{8,9},{9,10},{10,1... | collective-permute-start | bytes 196616 | tf_op jit(solution)/shard_map/ppermute | solution.py:40
  785.2 0.8 copy-start.4
  789.0 1.5 copy-start.5
  789.0 1.5 copy-start.9
Sparse Core Ops, SparseCore 0:
  29.5 362.8 all-gather.6
  394.2 385.8 all-gather.4
where the time goes:
time: 804 us; the launch traced here: 803 us
  waiting for transfers between devices  684 us (85%)
  starting transfers between devices  45.3 us (6%)
  matrix products  26.7 us (3%)
  other arithmetic  17.7 us (2%)
  local copies, waits for them, and re-layouts  15.2 us (2%)
  between operations  14.4 us (2%)
    all_gather x1, waiting for transfers between devices, on_device(): lax.all_gather(w_query[0], 'ep', axis=0, tiled=True)  373 us
    all_to_all x1, waiting for transfers between devices, on_device(): lax.all_to_all(spread, 'ep', split_axis=0, concat_axis=0, tiled=True)  108 us
    ppermute x8, waiting for transfers between devices, passed_along_2(): lax.ppermute(value, axis, [(source, source + steps) for source in range(l...  87.2 us
    all_gather x1, waiting for transfers between devices, on_device(): lax.all_gather(w_keyval[0], 'ep', axis=0, tiled=True)  78.5 us
    ppermute x1, waiting for transfers between devices, passed_along(): return lax.ppermute(block, axis, route)  27.8 us
    ppermute x8, starting transfers between devices, passed_along_2(): lax.ppermute(value, axis, [(source, source + steps) for source in range(l...  26.2 us
  transfers between devices with their start and end apart: 13, of which 8 were waited for; matrix products, arithmetic and copies ran while one was open for 6% of the time, Pallas kernels for 0%

commit v1 on v0

--- a/solution.py
+++ b/solution.py
@@ -128,7 +128,9 @@
     head_count = query_width // head_dim
     query_raw = jnp.dot(
         lifted,
-        lax.all_gather(w_query[0], "ep", axis=0, tiled=True),
+        jnp.concatenate(
+            lax.all_to_all(jnp.stack([w_query[0]] * lax.axis_size("ep")), "ep", 0, 0), axis=0
+        ),
         preferred_element_type=jnp.float32,
     )
     keyval_raw = jnp.dot(

time: 804 us -> 661 us (0.82); the launches traced: 803 us -> 652 us
  waiting for transfers between devices: 684 us -> 340 us
  blocking collectives: 0 us -> 209 us
  starting transfers between devices: 45.3 us -> 26.9 us
    all_gather x1 -> x0, waiting for transfers between devices: 373 us -> none  [on_device(): lax.all_gather(w_query[0], 'ep', axis=0, tiled=True)]
    all_to_all x0 -> x2, blocking collectives: none -> 209 us  [the longest x1 108 us: on_device(): lax.all_to_all(spread, 'ep', split_axis=0, concat_axis=0, tiled=True)]
    all_to_all x2 -> x1, waiting for transfers between devices: 116 us -> 0.01 us  [on_device(): lax.all_to_all(jnp.stack([w_query[0]] * lax.axis_size('ep')), 'ep', 0, 0)]
    ppermute x8, waiting for transfers between devices: 87.2 us -> 201 us  [passed_along_2(): lax.ppermute(value, axis, [(source, source + steps) for source in range(l...]
    all_gather x1, waiting for transfers between devices: 78.5 us -> 130 us  [on_device(): lax.all_gather(w_keyval[0], 'ep', axis=0, tiled=True)]
    ppermute x1, waiting for transfers between devices: 27.8 us -> 9.49 us  [passed_along(): return lax.ppermute(block, axis, route)]
    all_to_all x2 -> x1, starting transfers between devices: 18.7 us -> 6.43 us  [on_device(): lax.all_to_all(jnp.stack([w_query[0]] * lax.axis_size('ep')), 'ep', 0, 0)]
    dot_general x0 -> x1, local copies, waits for them, and re-layouts: none -> 11.7 us  [on_device(): jnp.dot(lifted, jnp.concatenate(lax.all_to_all(jnp.stack([w_query[0]] * l...]
  transfers between devices with their start and end apart: 13 -> 11, of which waited for: 8 -> 5; matrix products, arithmetic and copies ran while one was open for 6% -> 5% of each run, Pallas kernels for 0% -> 0%
where the time goes in v1:
time: 661 us; the launch traced here: 652 us
  waiting for transfers between devices  340 us (51%)
  blocking collectives  209 us (32%)
  starting transfers between devices  26.9 us (4%)
  matrix products  24.7 us (4%)
  local copies, waits for them, and re-layouts  22.6 us (3%)
  between operations  14.5 us (2%)
  other arithmetic  14.2 us (2%)
    ppermute x8, waiting for transfers between devices, passed_along_2(): lax.ppermute(value, axis, [(source, source + steps) for source in range(l...  201 us
    all_gather x1, waiting for transfers between devices, on_device(): lax.all_gather(w_keyval[0], 'ep', axis=0, tiled=True)  130 us
    all_to_all x1, blocking collectives, on_device(): lax.all_to_all(spread, 'ep', split_axis=0, concat_axis=0, tiled=True)  108 us
    all_to_all x1, blocking collectives, on_device(): lax.all_to_all(partial_out.astype(jnp.bfloat16), 'ep', split_axis=0, conc...  101 us
    ppermute x8, starting transfers between devices, passed_along_2(): lax.ppermute(value, axis, [(source, source + steps) for source in range(l...  20.4 us
  transfers between devices with their start and end apart: 11, of which 5 were waited for; matrix products, arithmetic and copies ran while one was open for 5% of the time, Pallas kernels for 0%

profile of v1, /device:TPU:32, one launch (start us, length us, event | category | flops | bytes accessed | tf_op | source)
XLA Modules:
  0.0 652.2 jit_solution(13211934177650480317)
XLA Ops:
  7.2 0.9 fusion.83
  8.0 0.8 fusion.78
  8.8 1.5 fusion.13
  10.4 0.1 fusion.74
  10.5 0.2 reduce_window_sum.11
  10.6 0.2 select_reduce_fusion
  10.8 1.7 fusion
  12.6 0.5 broadcast_in_dim.108
  13.1 107.7 %all_to_all.15 = bf16[64,8,4096]{2,1,0:T(8,128)(2,1)S(1)} all-to-all(bf16[64,8,4096]{2,1,0:T(8,128)(2,1)S(1)} %bitcast.116), channel_id=1, replica_groups=mesh['section'=4,'ep'=64] {'ep'}, dimensions={0} | all-to-all | bytes 8388608 | tf_op jit(solution)/shard_map/all_to_all | solution.py:111
  120.8 2.0 copy-done.4
  122.8 3.2 fusion.3
  126.0 9.7 %convolution_convert_fusion = bf16[64,8,4096]{2,1,0:T(8,128)(2,1)} fusion(bf16[1,1,384,4096]{3,2,1,0:T(8,128)(2,1)S(1)} %copy-done, bf16[1,1,4096,384]{3,2,1,0:T(8,128)(2,1)} %param.15, bf16[64,8,4096]{2,1,0:T(8,128)(2,1)} %copy-done.4, f32[512,384]{1,0:T(8,128)} %fusion.3), kind=kOutput, calls=%fused_computation.2 | convolution fusion | flops 3224502272 | bytes 15466496 | tf_op jit(solution)/shard_map/dot_general | solution.py:61
  135.7 101.0 %all_to_all.16 = bf16[64,8,4096]{2,1,0:T(8,128)(2,1)} all-to-all(bf16[64,8,4096]{2,1,0:T(8,128)(2,1)} %convolution_convert_fusion), channel_id=1, replica_groups=mesh['section'=4,'ep'=64] {'ep'}, dimensions={0} | all-to-all | bytes 8388608 | tf_op jit(solution)/shard_map/all_to_all | solution.py:115
  236.8 4.3 stack.3
  241.1 6.4 all-to-all-start.2
  247.5 3.4 collective-permute-start.3
  250.9 4.3 collective-permute-start.2
  255.2 3.4 collective-permute-start.1
  258.6 3.6 collective-permute-start
  262.3 19.4 %collective-permute-done = s32[128]{0:T(128)S(1)} collective-permute-done((s32[128]{0:T(128)S(1)}, s32[128]{0:T(128)S(1)}, u32[]{:S(2)}, u32[]{:S(2)}) %collective-permute-start) | collective-permute-done | bytes 544 | tf_op jit(solution)/shard_map/ppermute | solution.py:40
  281.8 62.0 %collective-permute-done.1 = s32[128]{0:T(128)S(1)} collective-permute-done((s32[128]{0:T(128)S(1)}, s32[128]{0:T(128)S(1)}, u32[]{:S(2)}, u32[]{:S(2)}) %collective-permute-start.1) | collective-permute-done | bytes 544 | tf_op jit(solution)/shard_map/ppermute | solution.py:40
  343.8 119.2 %collective-permute-done.2 = s32[128]{0:T(128)S(1)} collective-permute-done((s32[128]{0:T(128)S(1)}, s32[128]{0:T(128)S(1)}, u32[]{:S(2)}, u32[]{:S(2)}) %collective-permute-start.2) | collective-permute-done | bytes 544 | tf_op jit(solution)/shard_map/ppermute | solution.py:40
  463.1 0.2 fusion.65
  463.3 0.3 multiply_cosine_fusion
  463.6 3.2 convert_reduce_fusion
  466.8 2.6 gather_fusion
  469.4 3.1 fusion.15
  472.5 0.1 compare_and_fusion
  472.6 11.7 %copy.19 = bf16[1024,4096]{1,0:T(8,128)(2,1)} copy(bf16[1024,4096]{0,1:T(8,128)(2,1)} %bitcast.18) | data formatting | bytes 16777216 | tf_op jit(solution)/shard_map/dot_general | solution.py:129
  484.3 1.5 fusion.16
  485.8 9.5 %collective-permute-done.4 = bf16[128,4096]{1,0:T(8,128)(2,1)} collective-permute-done((bf16[128,4096]{1,0:T(8,128)(2,1)}, bf16[128,4096]{1,0:T(8,128)(2,1)}, u32[]{:S(2)}, u32[]{:S(2)}) %collective-permute-start.4) | collective-permute-done | bytes 1048608 | tf_op jit(solution)/shard_map/ppermute | solution.py:17
  495.3 1.5 fusion.17
  496.8 130.2 %all-gather.3.cloned.1.call-done = bf16[1,4096,256]{2,1,0:T(8,128)(2,1)} async-done(((bf16[1,64,256]{2,1,0:T(8,128)(2,1)}), bf16[1,4096,256]{2,1,0:T(8,128)(2,1)}) %all-gather.3.cloned.1.call-update) | async-done | bytes 2097168 | tf_op jit(solution)/shard_map/all_gather | solution.py:138
  627.1 2.4 fusion.19
  629.5 0.1 multiply_reduce_fusion.1
  629.8 0.1 fusion.72
  630.0 1.9 collective-permute-start.8
  631.9 1.3 collective-permute-start.7
  633.2 1.3 collective-permute-start.6
  634.5 1.3 collective-permute-start.5
  635.8 6.1 multiply_reduce_fusion
  642.0 0.1 multiply_multiply_fusion
  642.1 0.1 copy.20
  642.2 0.1 copy.21
  642.5 0.9 fusion.11
  643.4 0.6 fusion.41
  644.0 0.9 copy.24
  644.8 0.5 copy-done.1
  (59 shorter events, 0.5 us)
Async XLA Ops:
  7.2 118.9 %copy-start = (bf16[1,1,384,4096]{3,2,1,0:T(8,128)(2,1)S(1)}, bf16[1,1,384,4096]{3,2,1,0:T(8,128)(2,1)}, u32[]{:S(2)}) copy-start(bf16[1,1,384,4096]{3,2,1,0:T(8,128)(2,1)} %param.16) | copy-start | bytes 9437188
  13.1 109.7 %copy-start.11 = (bf16[1,1,4096,384]{3,2,1,0:T(8,128)(2,1)S(1)}, bf16[1,1,4096,384]{3,2,1,0:T(8,128)(2,1)}, u32[]{:S(2)}) copy-start(bf16[1,1,4096,384]{3,2,1,0:T(8,128)(2,1)} %param.14) | copy-start | bytes 9437188
  120.8 2.0 copy-start.4
  135.7 101.1 %copy-start.5 = (bf16[1,64,1024]{2,1,0:T(8,128)(2,1)S(1)}, bf16[1,64,1024]{2,1,0:T(8,128)(2,1)}, u32[]{:S(2)}) copy-start(bf16[1,64,1024]{2,1,0:T(8,128)(2,1)} %param.17) | copy-start | bytes 393220
  241.0 6.5 copy-start.8
  241.0 21.2 %copy-start.6 = (s32[1,128,8]{1,2,0:T(8,128)S(1)}, s32[1,128,8]{1,2,0:T(8,128)}, u32[]{:S(2)}) copy-start(s32[1,128,8]{1,2,0:T(8,128)} %param.12) | copy-start | bytes 12292
  241.0 21.2 %copy-start.7 = (f32[1,128,8]{1,2,0:T(8,128)S(1)}, f32[1,128,8]{1,2,0:T(8,128)}, u32[]{:S(2)}) copy-start(f32[1,128,8]{1,2,0:T(8,128)} %param.13) | copy-start | bytes 12292
  241.1 231.6 %all-to-all-start.2 = ((bf16[64,64,1024]{2,1,0:T(8,128)(2,1)}), bf16[64,64,1024]{2,1,0:T(8,128)(2,1)}, u32[]{:S(2)}, u32[]{:S(2)}) async-start(bf16[64,64,1024]{2,1,0:T(8,128)(2,1)} %stack.3), calls=%async_computation.2 | async-start | bytes 16777216 | tf_op jit(solution)/shard_map/all_to_all | solution.py:132
  247.5 379.6 %all-gather.3.cloned.1.call-start = ((), (), s32[]{:S(2)}) async-start(), calls=%async_computation.3 | async-start | bytes 2129920 | tf_op jit(solution)/shard_map/all_gather | solution.py:138
  247.5 215.5 %collective-permute-start.3 = (s32[128]{0:T(128)S(1)}, s32[128]{0:T(128)S(1)}, u32[]{:S(2)}, u32[]{:S(2)}) collective-permute-start(s32[128]{0:T(128)S(1)} %bitcast.119), channel_id=1, source_target_pairs={{0,1},{1,2},{2,3},{3,4},{4,5},{5,6},{6,7},{7,8},{8,9},{9,10},{10,1... | collective-permute-start | bytes 1544 | tf_op jit(solution)/shard_map/ppermute | solution.py:40
  250.9 212.1 %collective-permute-start.2 = (s32[128]{0:T(128)S(1)}, s32[128]{0:T(128)S(1)}, u32[]{:S(2)}, u32[]{:S(2)}) collective-permute-start(s32[128]{0:T(128)S(1)} %bitcast.120), channel_id=1, source_target_pairs={{0,2},{1,3},{2,4},{3,5},{4,6},{5,7},{6,8},{7,9},{8,10},{9,11},{10,... | collective-permute-start | bytes 1544 | tf_op jit(solution)/shard_map/ppermute | solution.py:40
  255.2 88.6 %collective-permute-start.1 = (s32[128]{0:T(128)S(1)}, s32[128]{0:T(128)S(1)}, u32[]{:S(2)}, u32[]{:S(2)}) collective-permute-start(s32[128]{0:T(128)S(1)} %bitcast.121), channel_id=1, source_target_pairs={{0,3},{1,4},{2,5},{3,6},{4,7},{5,8},{6,9},{7,10},{8,11},{9,12},{10... | collective-permute-start | bytes 1544 | tf_op jit(solution)/shard_map/ppermute | solution.py:40
  258.6 23.1 %collective-permute-start = (s32[128]{0:T(128)S(1)}, s32[128]{0:T(128)S(1)}, u32[]{:S(2)}, u32[]{:S(2)}) collective-permute-start(s32[128]{0:T(128)S(1)} %bitcast.122), channel_id=1, source_target_pairs={{0,4},{1,5},{2,6},{3,7},{4,8},{5,9},{6,10},{7,11},{8,12},{9,13},{1... | collective-permute-start | bytes 1544 | tf_op jit(solution)/shard_map/ppermute | solution.py:40
  466.8 2.6 copy-start.3
  472.5 22.8 %collective-permute-start.4 = (bf16[128,4096]{1,0:T(8,128)(2,1)}, bf16[128,4096]{1,0:T(8,128)(2,1)}, u32[]{:S(2)}, u32[]{:S(2)}) collective-permute-start(bf16[128,4096]{1,0:T(8,128)(2,1)} %fusion.15), channel_id=1, source_target_pairs={{192,0},{0,64},{64,128},{128,192},{193,1},{1,65},{65,129},{129,193... | collective-permute-start | bytes 3145736 | tf_op jit(solution)/shard_map/ppermute | solution.py:17
  472.6 11.7 %copy-start.2 = (f32[128,4096]{1,0:T(8,128)S(1)}, f32[128,4096]{1,0:T(8,128)}, u32[]{:S(2)}) copy-start(f32[128,4096]{1,0:T(8,128)} %gather_fusion) | copy-start | bytes 6291460
  485.8 143.8 %copy-start.9 = (f32[1,128]{1,0:T(1,128)S(1)}, f32[1,128]{1,0:T(1,128)}, u32[]{:S(2)}) copy-start(f32[1,128]{1,0:T(1,128)} %param.20) | copy-start | bytes 1540
  630.0 12.4 %collective-permute-start.8 = (bf16[128,256]{1,0:T(8,128)(2,1)S(1)}, bf16[128,256]{1,0:T(8,128)(2,1)S(1)}, u32[]{:S(2)}, u32[]{:S(2)}) collective-permute-start(bf16[128,256]{1,0:T(8,128)(2,1)S(1)} %pad_maximum_fusion.2), channel_id=1, source_target_pairs={{0,1},{1,2},{2,3},{3,4},{4,5},{5,6},{6,7},{7,8},{8,9},{9,10},{10,1... | collective-permute-start | bytes 196616 | tf_op jit(solution)/shard_map/ppermute | solution.py:40
  631.9 10.5 %collective-permute-start.7 = (bf16[128,256]{1,0:T(8,128)(2,1)S(1)}, bf16[128,256]{1,0:T(8,128)(2,1)S(1)}, u32[]{:S(2)}, u32[]{:S(2)}) collective-permute-start(bf16[128,256]{1,0:T(8,128)(2,1)S(1)} %pad_maximum_fusion.2), channel_id=1, source_target_pairs={{0,2},{1,3},{2,4},{3,5},{4,6},{5,7},{6,8},{7,9},{8,10},{9,11},{10,... | collective-permute-start | bytes 196616 | tf_op jit(solution)/shard_map/ppermute | solution.py:40
  633.2 9.2 %collective-permute-start.6 = (bf16[128,256]{1,0:T(8,128)(2,1)S(1)}, bf16[128,256]{1,0:T(8,128)(2,1)S(1)}, u32[]{:S(2)}, u32[]{:S(2)}) collective-permute-start(bf16[128,256]{1,0:T(8,128)(2,1)S(1)} %pad_maximum_fusion.2), channel_id=1, source_target_pairs={{0,3},{1,4},{2,5},{3,6},{4,7},{5,8},{6,9},{7,10},{8,11},{9,12},{10... | collective-permute-start | bytes 196616 | tf_op jit(solution)/shard_map/ppermute | solution.py:40
  634.5 7.8 %collective-permute-start.5 = (bf16[128,256]{1,0:T(8,128)(2,1)S(1)}, bf16[128,256]{1,0:T(8,128)(2,1)S(1)}, u32[]{:S(2)}, u32[]{:S(2)}) collective-permute-start(bf16[128,256]{1,0:T(8,128)(2,1)S(1)} %pad_maximum_fusion.2), channel_id=1, source_target_pairs={{0,4},{1,5},{2,6},{3,7},{4,8},{5,9},{6,10},{7,11},{8,12},{9,13},{1... | collective-permute-start | bytes 196616 | tf_op jit(solution)/shard_map/ppermute | solution.py:40
  635.8 6.2 copy-start.10
  643.4 2.0 copy-start.1
Sparse Core Ops, SparseCore 0:
  262.4 364.6 all-gather.2
